TPU v7x, 512 devices: a whole 4x8x8 slice. The times are simulated.
512 devices in a mesh: dp: 16 (over y, core), tensor: 32 (over z, x).
Axes of the slice: x: 4, y: 8, z: 8, core: 2. Of those that a mesh axis runs over, the one named last changes fastest.
Arguments:
- layer_input: bfloat16 [65536, 8192], P('dp', 'tensor'), may hold values from -6 to 6
- output_grad: bfloat16 [65536, 1024], P(('dp', 'tensor')), may hold values from -6 to 6
- key_weight: bfloat16 [8192, 1024], P('tensor'), may hold values from -0.0625 to 0.0625
- adapter_down: bfloat16 [128, 16, 8192], P('dp', None, 'tensor'), may hold values from -0.0625 to 0.0625
- adapter_up: bfloat16 [128, 16, 1024], P('dp', None, 'tensor'), may hold values from -0.1875 to 0.1875
- segment_adapter: int32 [512], replicated, may hold values from 0 to 127
- adapter_slot: int32 [128], replicated, may hold values from 0 to 127, each once
- live_segments: int32 [16], P('dp'), may hold values from 1 to 32, as said below
Outputs:
- input_grad: bfloat16 [65536, 8192], P('dp', 'tensor')
- down_grad: bfloat16 [128, 16, 8192], P('dp', None, 'tensor')
- up_grad: bfloat16 [128, 16, 1024], P('dp', None, 'tensor')
Inputs may be any that keep to these rules, and one draw needn't show every extreme that they name: `live_segments`: some data group has all 32 segments live; a group's segments at or past its count are padding.
All inputs are finite; a program needn't handle non-finite values.
Results may differ from a plain program's by a relative error of at most 0.0057.
Values may be sent and summed in bfloat16 or wider, within the bound.
No kernel may reach another device: no remote copies, remote signals or barrier semaphores. Data moves between devices by JAX's collectives and lax.ppermute only.
A program may use at most 64 MiB of HBM per device.

v0:
```python
import jax
import jax.numpy as jnp
from jax import lax
from jax.sharding import PartitionSpec as P


def on_device(
    layer_input,
    output_grad,
    key_weight,
    adapter_down,
    adapter_up,
    segment_adapter,
    adapter_slot,
    live_segments,
):
    tensor_size = lax.axis_size("tensor")
    position = lax.axis_index("tensor")
    group_count = lax.axis_size("dp")
    group_index = lax.axis_index("dp")
    row_count = output_grad.shape[0]
    tok_group = layer_input.shape[0]
    width_shard = layer_input.shape[1]
    key_width = output_grad.shape[1]
    key_shard = key_width // tensor_size
    adapters = adapter_slot.shape[0]
    rank_dim = adapter_down.shape[1]
    per_owner = adapter_down.shape[0]
    seg_total = segment_adapter.shape[0]
    seg_group = seg_total // group_count
    seg_len = tok_group // seg_group
    f32 = jnp.float32
    bf16 = jnp.bfloat16
    whole_raw = lax.all_gather(output_grad, "tensor", axis=0, tiled=True)
    slot_ids = jnp.arange(adapters, dtype=jnp.int32)
    lookup = segment_adapter[:, None] == slot_ids[None, :]
    every_slot = jnp.sum(jnp.where(lookup, adapter_slot[None, :], 0), axis=1)
    seg_slot = lax.dynamic_slice_in_dim(every_slot, group_index * seg_group, seg_group)
    seg_live = jnp.arange(seg_group, dtype=jnp.int32) < live_segments[0]
    local_store = jnp.concatenate([adapter_down, adapter_up], axis=2).reshape(per_owner, -1)
    spread = jnp.broadcast_to(local_store[None], (group_count,) + local_store.shape)
    stores = lax.all_to_all(spread, "dp", 0, 0, tiled=True).reshape(adapters, -1)
    choose = (seg_slot[:, None] == slot_ids[None, :]).astype(bf16)
    seg_store = jnp.dot(choose, stores, preferred_element_type=f32).astype(bf16)
    seg_store = seg_store.reshape(seg_group, rank_dim, width_shard + key_shard)
    down_seg = seg_store[:, :, :width_shard]
    up_seg = seg_store[:, :, width_shard:]
    input_seg = layer_input.reshape(seg_group, seg_len, width_shard)
    proj_part = jnp.einsum("sjd,srd->srj", input_seg, down_seg, preferred_element_type=f32)
    first = jnp.concatenate([proj_part, up_seg.astype(f32)], axis=2).reshape(seg_group, -1)
    first = lax.all_to_all(first, "tensor", 0, 0, tiled=True)
    first = first.reshape(tensor_size, rank_dim, seg_len + key_shard)
    projected_own = jnp.sum(first[:, :, :seg_len], axis=0).astype(bf16)
    up_own = jnp.transpose(first[:, :, seg_len:], (1, 0, 2)).reshape(rank_dim, key_width)
    up_own = up_own.astype(bf16)
    own_live = position < live_segments[0]
    masked_own = jnp.where(own_live, output_grad, jnp.zeros_like(output_grad))
    lowrank_own = lax.dot_general(
        up_own, masked_own, (((1,), (1,)), ((), ())), preferred_element_type=f32
    ).astype(bf16)
    seg_up_own = 2.0 * jnp.dot(projected_own, masked_own, preferred_element_type=f32)
    low_spread = jnp.broadcast_to(
        lowrank_own.reshape(1, row_count * rank_dim), (tensor_size, row_count * rank_dim)
    )
    up_pieces = jnp.transpose(
        seg_up_own.reshape(rank_dim, tensor_size, key_shard), (1, 0, 2)
    ).reshape(tensor_size, rank_dim * key_shard)
    up_round = lax.reduce_precision(up_pieces, exponent_bits=8, mantissa_bits=7)
    up_high = up_round.astype(bf16)
    up_low = (up_pieces - up_round).astype(bf16)
    second = jnp.concatenate([low_spread, up_high, up_low], axis=1)
    second = second.reshape(tensor_size, -1, 128)
    second = lax.all_to_all(second, "tensor", 0, 0, tiled=True).reshape(tensor_size, -1)
    lowrank = second[:, : row_count * rank_dim].reshape(seg_group, rank_dim, seg_len)
    piece = rank_dim * key_shard
    low_end = row_count * rank_dim
    seg_up = second[:, low_end : low_end + piece].astype(f32)
    seg_up = seg_up + second[:, low_end + piece :].astype(f32)
    seg_up = seg_up.reshape(seg_group, rank_dim, key_shard)
    seg_down = 2.0 * jnp.einsum("srj,sjd->srd", lowrank, input_seg, preferred_element_type=f32)
    seg_grad = jnp.concatenate([seg_down, seg_up], axis=2)
    onehot = (slot_ids[:, None] == seg_slot[None, :]).astype(bf16)
    grad_round = lax.reduce_precision(seg_grad, exponent_bits=8, mantissa_bits=7)
    grad_high = grad_round.astype(bf16)
    grad_low = (seg_grad - grad_round).astype(bf16)
    flat_high = grad_high.reshape(seg_group, -1)
    flat_low = grad_low.reshape(seg_group, -1)
    part = jnp.dot(onehot, flat_high, preferred_element_type=f32)
    part = part + jnp.dot(onehot, flat_low, preferred_element_type=f32)
    part = part.astype(bf16).reshape(group_count, per_owner, -1)
    gathered = lax.all_to_all(part, "dp", 0, 0, tiled=True)
    frozen = lax.dot_general(
        whole_raw, key_weight, (((1,), (1,)), ((), ())), preferred_element_type=f32
    )
    frozen = jnp.where(jnp.repeat(seg_live, seg_len)[:, None], frozen, jnp.zeros_like(frozen))
    extra = jnp.einsum("srj,srd->sjd", lowrank, down_seg, preferred_element_type=f32)
    input_grad = (frozen + 2.0 * extra.reshape(tok_group, width_shard)).astype(bf16)
    gathered, input_grad = lax.optimization_barrier((gathered, input_grad))
    total = jnp.sum(gathered.astype(f32), axis=0).reshape(per_owner, rank_dim, -1)
    down_grad = total[:, :, :width_shard].astype(bf16)
    up_grad = total[:, :, width_shard:].astype(bf16)
    return (input_grad, down_grad, up_grad)


def solution(mesh):
    in_specs = (
        P("dp", "tensor"),
        P(("dp", "tensor"), None),
        P("tensor", None),
        P("dp", None, "tensor"),
        P("dp", None, "tensor"),
        P(),
        P(),
        P("dp"),
    )
    out_specs = (P("dp", "tensor"), P("dp", None, "tensor"), P("dp", None, "tensor"))
    return jax.shard_map(
        on_device, mesh=mesh, in_specs=in_specs, out_specs=out_specs, check_vma=False
    )
```

profile of v0, /device:TPU:1, one launch (start us, length us, event | category | flops | bytes accessed | tf_op | source)
XLA Modules:
  0.0 147.1 jit_solution(13841824733136216324)
XLA Ops:
  7.2 0.0 copy-start
  7.2 0.0 copy-start.5
  7.2 0.0 copy-start.6
  7.2 0.0 all-gather.2.cloned.1.call-start
  7.2 0.7 all-gather.2.cloned.1.call-update
  7.9 0.9 pad_maximum_fusion.2
  8.8 0.1 broadcast_in_dim.54
  9.0 1.1 broadcast_in_dim.55
  10.0 10.4 %all-to-all-start = ((bf16[16,8,4608]{2,1,0:T(8,128)(2,1)}), bf16[16,8,4608]{2,1,0:T(8,128)(2,1)S(1)}, u32[]{:S(2)}, u32[]{:S(2)}) async-start(bf16[16,8,4608]{2,1,0:T(8,128)(2,1)} %broadcast_in_dim.55), calls=%async_computation | async-start | bytes 2359296 | tf_op jit(solution)/shard_map/all_to_all | solution.py:42
  20.4 0.0 copy-done.5
  20.4 0.0 copy-done.6
  20.4 0.2 select_reduce_fusion
  20.7 0.1 dynamic_slice.3
  20.7 30.3 %all-to-all-done = bf16[16,8,4608]{2,1,0:T(8,128)(2,1)S(1)} async-done(((bf16[16,8,4608]{2,1,0:T(8,128)(2,1)}), bf16[16,8,4608]{2,1,0:T(8,128)(2,1)S(1)}, u32[]{:S(2)}, u32[]{:S(2)}) %all-to-all-start) | async-done | bytes 1179680 | tf_op jit(solution)/shard_map/all_to_all | solution.py:42
  51.0 1.1 convolution_convert_fusion
  52.1 1.5 %reshape.65 = bf16[32,16,288]{2,1,0:T(8,128)(2,1)S(1)} reshape(bf16[32,4608]{1,0:T(8,128)(2,1)} %convolution_convert_fusion) | data formatting | bytes 589824 | tf_op jit(solution)/shard_map/reshape | solution.py:45
  53.6 0.0 copy-start.1
  53.6 0.0 copy-done
  53.7 0.6 fusion.10
  54.3 0.0 copy-start.4
  54.3 0.1 pad_maximum_fusion.1
  54.4 1.4 all_to_all.20
  55.8 0.0 copy-done.1
  55.8 11.1 %all-to-all-start.1 = ((f32[32,1,2560]{2,1,0:T(1,128)}), f32[32,1,2560]{2,1,0:T(1,128)S(1)}, u32[]{:S(2)}, u32[]{:S(2)}) async-start(f32[32,1,2560]{2,1,0:T(1,128)} %all_to_all.20), calls=%async_computation.1 | async-start | bytes 655360 | tf_op jit(solution)/shard_map/all_to_all | solution.py:51
  67.5 13.1 %all-to-all-done.1 = f32[32,1,2560]{2,1,0:T(1,128)S(1)} async-done(((f32[32,1,2560]{2,1,0:T(1,128)}), f32[32,1,2560]{2,1,0:T(1,128)S(1)}, u32[]{:S(2)}, u32[]{:S(2)}) %all-to-all-start.1) | async-done | bytes 327712 | tf_op jit(solution)/shard_map/all_to_all | solution.py:51
  80.6 0.8 reduce.1
  81.4 0.3 reshape.67
  81.7 0.0 copy-done.4
  81.7 0.2 convolution_multiply_fusion.2
  81.9 0.1 reshape.68
  82.0 0.2 copy.25
  82.2 0.1 reshape.69
  82.4 0.2 convert_element_type.55
  82.6 0.2 fusion.5
  82.8 16.6 %all_to_all.25 = bf16[32,24,128]{2,1,0:T(8,128)(2,1)S(1)} all-to-all(bf16[32,24,128]{2,1,0:T(8,128)(2,1)S(1)} %bitcast.45), channel_id=1, replica_groups=mesh['dp'=16,'tensor'=32] {'tensor'}, dimensions={0} | all-to-all | bytes 393216 | tf_op jit(solution)/shard_map/all_to_all | solution.py:73
  99.5 0.0 copy-start.2
  99.6 0.1 reshape.73
  99.7 0.4 convolution_multiply_fusion.1
  100.1 0.1 copy-done.2
  100.2 0.1 pad_maximum_fusion
  100.2 0.3 concatenate.18
  100.6 0.4 fusion.8
  101.0 0.0 copy-start.3
  101.0 1.6 %fusion.1 = bf16[16,8,4608]{2,1,0:T(8,128)(2,1)} fusion(f32[128,4608]{1,0:T(8,128)S(1)} %fusion.8, f32[32,4608]{1,0:T(8,128)S(1)} %concatenate.18, s32[32]{0:T(128)S(1)} %dynamic_slice.3), kind=kOutput, calls=%fused_computation.2 | convolution fusion | flops 39374848 | bytes 4128896 | tf_op jit(solution)/shard_map/dot_general | solution.py:89
  102.6 5.5 %all-to-all-start.3 = ((bf16[16,8,4608]{2,1,0:T(8,128)(2,1)}), bf16[16,8,4608]{2,1,0:T(8,128)(2,1)S(1)}, u32[]{:S(2)}, u32[]{:S(2)}) async-start(bf16[16,8,4608]{2,1,0:T(8,128)(2,1)} %fusion.1), calls=%async_computation.3 | async-start | bytes 2359296 | tf_op jit(solution)/shard_map/all_to_all | solution.py:91
  108.1 0.1 broadcast_bitcast_fusion
  108.2 0.0 copy-done.3
  108.2 3.7 %convolution_multiply_fusion = f32[32,128,256]{2,1,0:T(8,128)} fusion(bf16[32,16,128]{2,1,0:T(8,128)(2,1)S(1)} %bitcast.41, bf16[32,16,288]{2,1,0:T(8,128)(2,1)} %copy-done.1), kind=kOutput, calls=%fused_computation.7 | convolution fusion | flops 34603008 | bytes 4587520 | tf_op jit(solution)/shard_map/srj,srd->sjd/dot_general | solution.py:96
  111.8 13.0 %all-gather.2.cloned.1.call-done = bf16[4096,1024]{1,0:T(8,128)(2,1)} async-done(((bf16[128,1024]{1,0:T(8,128)(2,1)}), bf16[4096,1024]{1,0:T(8,128)(2,1)}) %all-gather.2.cloned.1.call-update) | async-done | bytes 8388624 | tf_op jit(solution)/shard_map/all_gather | solution.py:34
  124.9 7.1 %fusion.3 = bf16[4096,256]{1,0:T(8,128)(2,1)} fusion(f32[4096,256]{1,0:T(8,128)} %bitcast.39, bf16[4096,1024]{1,0:T(8,128)(2,1)} %all-gather.2.cloned.1.call-done, bf16[256,1024]{1,0:T(8,128)(2,1)} %param.10, pred[4096]{0:T(1024)(128)(4,1)S(1)} %broadcast_bitcast_fusion), kind=kOutput, calls=%fused_computation.6 | convolution fusion | flops 2150629376 | bytes 15208448 | tf_op jit(solution)/shard_map/dot_general | solution.py:92
  131.9 6.7 %all-to-all-done.3 = bf16[16,8,4608]{2,1,0:T(8,128)(2,1)S(1)} async-done(((bf16[16,8,4608]{2,1,0:T(8,128)(2,1)}), bf16[16,8,4608]{2,1,0:T(8,128)(2,1)S(1)}, u32[]{:S(2)}, u32[]{:S(2)}) %all-to-all-start.3) | async-done | bytes 1179680 | tf_op jit(solution)/shard_map/all_to_all | solution.py:91
  138.7 0.2 reduce
  138.8 0.2 reshape.76
  139.0 0.6 slice.46
  139.7 0.6 slice.47
  (13 shorter events, 0.3 us)
Async XLA Ops:
  7.2 46.5 %copy-start = (bf16[4096,256]{1,0:T(8,128)(2,1)S(1)}, bf16[4096,256]{1,0:T(8,128)(2,1)}, u32[]{:S(2)}) copy-start(bf16[4096,256]{1,0:T(8,128)(2,1)} %param.8) | copy-start | bytes 6291460
  7.2 13.2 %copy-start.5 = (s32[512]{0:T(512)S(1)}, s32[512]{0:T(512)}, u32[]{:S(2)}) copy-start(s32[512]{0:T(512)} %param.13) | copy-start | bytes 6148
  7.2 13.2 %copy-start.6 = (s32[128]{0:T(128)S(1)}, s32[128]{0:T(128)}, u32[]{:S(2)}) copy-start(s32[128]{0:T(128)} %param.14) | copy-start | bytes 1540
  7.2 117.7 %all-gather.2.cloned.1.call-start = ((), (), s32[]{:S(2)}) async-start(), calls=%async_computation.4 | async-start | bytes 8650752 | tf_op jit(solution)/shard_map/all_gather | solution.py:34
  10.0 41.0 %all-to-all-start = ((bf16[16,8,4608]{2,1,0:T(8,128)(2,1)}), bf16[16,8,4608]{2,1,0:T(8,128)(2,1)S(1)}, u32[]{:S(2)}, u32[]{:S(2)}) async-start(bf16[16,8,4608]{2,1,0:T(8,128)(2,1)} %broadcast_in_dim.55), calls=%async_computation | async-start | bytes 2359296 | tf_op jit(solution)/shard_map/all_to_all | solution.py:42
  53.6 2.2 %copy-start.1 = (bf16[32,16,288]{2,1,0:T(8,128)(2,1)}, bf16[32,16,288]{2,1,0:T(8,128)(2,1)S(1)}, u32[]{:S(2)}) copy-start(bf16[32,16,288]{2,1,0:T(8,128)(2,1)S(1)} %reshape.65) | copy-start | bytes 884740
  54.3 27.4 %copy-start.4 = (bf16[128,1024]{1,0:T(8,128)(2,1)S(1)}, bf16[128,1024]{1,0:T(8,128)(2,1)}, u32[]{:S(2)}) copy-start(bf16[128,1024]{1,0:T(8,128)(2,1)} %param.9) | copy-start | bytes 786436
  55.8 24.9 %all-to-all-start.1 = ((f32[32,1,2560]{2,1,0:T(1,128)}), f32[32,1,2560]{2,1,0:T(1,128)S(1)}, u32[]{:S(2)}, u32[]{:S(2)}) async-start(f32[32,1,2560]{2,1,0:T(1,128)} %all_to_all.20), calls=%async_computation.1 | async-start | bytes 655360 | tf_op jit(solution)/shard_map/all_to_all | solution.py:51
  99.5 0.6 copy-start.2
  101.0 7.1 %copy-start.3 = (bf16[4,8,16,128]{3,2,1,0:T(8,128)(2,1)S(1)}, bf16[4,8,16,128]{3,2,1,0:T(8,128)(2,1)}, u32[]{:S(2)}) copy-start(bf16[4,8,16,128]{3,2,1,0:T(8,128)(2,1)} %copy-done.2) | copy-start | bytes 393220
  102.6 36.1 %all-to-all-start.3 = ((bf16[16,8,4608]{2,1,0:T(8,128)(2,1)}), bf16[16,8,4608]{2,1,0:T(8,128)(2,1)S(1)}, u32[]{:S(2)}, u32[]{:S(2)}) async-start(bf16[16,8,4608]{2,1,0:T(8,128)(2,1)} %fusion.1), calls=%async_computation.3 | async-start | bytes 2359296 | tf_op jit(solution)/shard_map/all_to_all | solution.py:91
Sparse Core Ops, SparseCore 0:
  11.2 113.6 all-gather.1
where the time goes:
time: 148 us; the launch traced here: 147 us
  waiting for transfers between devices  63.8 us (43%)
  starting transfers between devices  27 us (18%)
  blocking collectives  16.6 us (11%)
  matrix products  15.2 us (10%)
  between operations  14.9 us (10%)
  local copies, waits for them, and re-layouts  7.34 us (5%)
  other arithmetic  2.28 us (2%)
    all_to_all x1, waiting for transfers between devices, on_device(): lax.all_to_all(spread, 'dp', 0, 0, tiled=True).reshape(adapters, -1)  30.3 us
    all_to_all x1, blocking collectives, on_device(): lax.all_to_all(second, 'tensor', 0, 0, tiled=True).reshape(tensor_size, -1)  16.6 us
    all_to_all x1, waiting for transfers between devices, on_device(): first = lax.all_to_all(first, 'tensor', 0, 0, tiled=True)  13.1 us
    all_gather x1, waiting for transfers between devices, on_device(): whole_raw = lax.all_gather(output_grad, 'tensor', axis=0, tiled=True)  13 us
    all_to_all x1, starting transfers between devices, on_device(): first = lax.all_to_all(first, 'tensor', 0, 0, tiled=True)  11.1 us
    all_to_all x1, starting transfers between devices, on_device(): lax.all_to_all(spread, 'dp', 0, 0, tiled=True).reshape(adapters, -1)  10.4 us
    dot_general x1, matrix products, on_device(): lax.dot_general(whole_raw, key_weight, (((1,), (1,)), ((), ())), preferre...  7.09 us
    all_to_all x1, waiting for transfers between devices, on_device(): gathered = lax.all_to_all(part, 'dp', 0, 0, tiled=True)  6.74 us
  transfers between devices with their start and end apart: 4, of which 4 were waited for; matrix products, arithmetic and copies ran while one was open for 15% of the time, Pallas kernels for 0%

commit v1 on v0

--- a/solution.py
+++ b/solution.py
@@ -2,6 +2,11 @@
 import jax.numpy as jnp
 from jax import lax
 from jax.sharding import PartitionSpec as P
+
+
+def gather_from_all(x, axis, dim):
+    copies = jnp.concatenate([x] * lax.axis_size(axis), axis=dim)
+    return lax.all_to_all(copies, axis, dim, dim, tiled=True)
 
 
 def on_device(
@@ -31,7 +36,7 @@
     seg_len = tok_group // seg_group
     f32 = jnp.float32
     bf16 = jnp.bfloat16
-    whole_raw = lax.all_gather(output_grad, "tensor", axis=0, tiled=True)
+    whole_raw = gather_from_all(output_grad, "tensor", 0)
     slot_ids = jnp.arange(adapters, dtype=jnp.int32)
     lookup = segment_adapter[:, None] == slot_ids[None, :]
     every_slot = jnp.sum(jnp.where(lookup, adapter_slot[None, :], 0), axis=1)

time: 148 us -> 325 us (2.20)
  waiting for transfers between devices: 63.8 us -> 229 us
  local copies, waits for them, and re-layouts: 7.34 us -> 41.7 us
  blocking collectives: 16.6 us -> 0 us
  between operations: 14.9 us -> 1.51 us
  starting transfers between devices: 27 us -> 35.5 us
    all_to_all x0 -> x2, waiting for transfers between devices: none -> 192 us  [the longest x1 185 us: gather_from_all(): return lax.all_to_all(copies, axis, dim, dim, tiled=True)]
    unnamed x18 -> x41, local copies, waits for them, and re-layouts: 0.22 us -> 31.8 us
    all_to_all x1, waiting for transfers between devices: 30.3 us -> 5.09 us  [on_device(): lax.all_to_all(spread, 'dp', 0, 0, tiled=True).reshape(adapters, -1)]
    all_to_all x1 -> x0, blocking collectives: 16.6 us -> none  [on_device(): lax.all_to_all(second, 'tensor', 0, 0, tiled=True).reshape(tensor_size, -1)]
    all_to_all x1, waiting for transfers between devices: 6.74 us -> 22.8 us  [on_device(): gathered = lax.all_to_all(part, 'dp', 0, 0, tiled=True)]
    all_gather x1 -> x0, waiting for transfers between devices: 13 us -> none  [on_device(): whole_raw = lax.all_gather(output_grad, 'tensor', axis=0, tiled=True)]
    all_to_all x0 -> x2, starting transfers between devices: none -> 9.08 us  [the longest x1 4.96 us: gather_from_all(): return lax.all_to_all(copies, axis, dim, dim, tiled=True)]
    all_to_all x1, waiting for transfers between devices: 13.1 us -> 8.75 us  [on_device(): first = lax.all_to_all(first, 'tensor', 0, 0, tiled=True)]
  transfers between devices with their start and end apart: 4 -> 5, of which waited for: 4 -> 5; matrix products, arithmetic and copies ran while one was open for 15% -> 14% of each run, Pallas kernels for 0% -> 0%
where the time goes in v1:
time: 325 us; the launch traced here: 324 us
  waiting for transfers between devices  229 us (70%)
  local copies, waits for them, and re-layouts  41.7 us (13%)
  starting transfers between devices  35.5 us (11%)
  matrix products  12.1 us (4%)
  other arithmetic  4.78 us (1%)
    all_to_all x1, waiting for transfers between devices, gather_from_all(): return lax.all_to_all(copies, axis, dim, dim, tiled=True)  185 us
    unnamed x41, local copies, waits for them, and re-layouts  31.8 us
    all_to_all x1, waiting for transfers between devices, on_device(): gathered = lax.all_to_all(part, 'dp', 0, 0, tiled=True)  22.8 us
    all_to_all x1, starting transfers between devices, on_device(): first = lax.all_to_all(first, 'tensor', 0, 0, tiled=True)  11.1 us
    all_to_all x1, starting transfers between devices, on_device(): lax.all_to_all(spread, 'dp', 0, 0, tiled=True).reshape(adapters, -1)  10.4 us
    all_to_all x1, waiting for transfers between devices, on_device(): first = lax.all_to_all(first, 'tensor', 0, 0, tiled=True)  8.75 us
    all_to_all x1, waiting for transfers between devices, on_device(): lax.all_to_all(second, 'tensor', 0, 0, tiled=True).reshape(tensor_size, -1)  7.72 us
  transfers between devices with their start and end apart: 5, of which 5 were waited for; matrix products, arithmetic and copies ran while one was open for 14% of the time, Pallas kernels for 0%

profile of v1, /device:TPU:1, one launch (start us, length us, event | category | flops | bytes accessed | tf_op | source)
XLA Modules:
  0.0 324.4 jit_solution(16047105888117839680)
XLA Ops:
  0.7 1.0 pad_maximum_fusion.2
  1.8 1.1 broadcast_in_dim.55
  2.9 10.4 %all-to-all-start = ((bf16[16,8,4608]{2,1,0:T(8,128)(2,1)}), bf16[16,8,4608]{2,1,0:T(8,128)(2,1)S(1)}, u32[]{:S(2)}, u32[]{:S(2)}) async-start(bf16[16,8,4608]{2,1,0:T(8,128)(2,1)} %broadcast_in_dim.55), calls=%async_computation | async-start | bytes 2359296 | tf_op jit(solution)/shard_map/all_to_all | solution.py:47
  13.3 1.7 constant_dynamic-update-slice_fusion.31
  15.0 1.7 constant_dynamic-update-slice_fusion.30
  16.7 1.7 constant_dynamic-update-slice_fusion.29
  18.3 0.9 select_reduce_fusion
  19.3 1.7 constant_dynamic-update-slice_fusion.28
  21.0 1.7 constant_dynamic-update-slice_fusion.27
  22.7 1.7 constant_dynamic-update-slice_fusion.26
  24.4 1.7 constant_dynamic-update-slice_fusion.25
  26.1 1.7 constant_dynamic-update-slice_fusion.24
  27.7 1.7 constant_dynamic-update-slice_fusion.23
  29.4 0.7 constant_dynamic-update-slice_fusion.22
  30.1 0.7 constant_dynamic-update-slice_fusion.21
  30.9 0.7 constant_dynamic-update-slice_fusion.20
  31.6 0.7 constant_dynamic-update-slice_fusion.19
  32.3 0.7 constant_dynamic-update-slice_fusion.18
  33.0 0.7 constant_dynamic-update-slice_fusion.17
  33.7 0.7 constant_dynamic-update-slice_fusion.16
  34.5 0.7 constant_dynamic-update-slice_fusion.15
  35.2 0.7 constant_dynamic-update-slice_fusion.14
  35.9 0.7 constant_dynamic-update-slice_fusion.13
  36.6 0.7 constant_dynamic-update-slice_fusion.12
  37.4 0.7 constant_dynamic-update-slice_fusion.11
  38.1 0.7 constant_dynamic-update-slice_fusion.10
  38.8 5.1 %all-to-all-done = bf16[16,8,4608]{2,1,0:T(8,128)(2,1)S(1)} async-done(((bf16[16,8,4608]{2,1,0:T(8,128)(2,1)}), bf16[16,8,4608]{2,1,0:T(8,128)(2,1)S(1)}, u32[]{:S(2)}, u32[]{:S(2)}) %all-to-all-start) | async-done | bytes 1179680 | tf_op jit(solution)/shard_map/all_to_all | solution.py:47
  43.9 1.1 convolution_convert_fusion
  45.0 1.5 reshape.67
  46.5 0.6 fusion.10
  47.2 1.4 all_to_all.31
  48.6 11.1 %all-to-all-start.1 = ((f32[32,1,2560]{2,1,0:T(1,128)}), f32[32,1,2560]{2,1,0:T(1,128)S(1)}, u32[]{:S(2)}, u32[]{:S(2)}) async-start(f32[32,1,2560]{2,1,0:T(1,128)} %all_to_all.31), calls=%async_computation.1 | async-start | bytes 655360 | tf_op jit(solution)/shard_map/all_to_all | solution.py:56
  59.7 0.7 constant_dynamic-update-slice_fusion.9
  61.1 0.7 constant_dynamic-update-slice_fusion.8
  61.8 0.7 constant_dynamic-update-slice_fusion.7
  62.5 0.7 constant_dynamic-update-slice_fusion.6
  63.3 0.7 constant_dynamic-update-slice_fusion.5
  64.0 0.7 constant_dynamic-update-slice_fusion.4
  64.7 8.7 %all-to-all-done.1 = f32[32,1,2560]{2,1,0:T(1,128)S(1)} async-done(((f32[32,1,2560]{2,1,0:T(1,128)}), f32[32,1,2560]{2,1,0:T(1,128)S(1)}, u32[]{:S(2)}, u32[]{:S(2)}) %all-to-all-start.1) | async-done | bytes 327712 | tf_op jit(solution)/shard_map/all_to_all | solution.py:56
  73.5 1.5 reduce.1
  75.0 1.3 reshape.69
  77.0 0.2 convert_element_type.55
  77.1 0.2 fusion.5
  77.4 0.7 copy.20
  78.1 4.1 %all-to-all-start.2 = ((bf16[32,24,128]{2,1,0:T(8,128)(2,1)}), bf16[32,24,128]{2,1,0:T(8,128)(2,1)S(1)}, u32[]{:S(2)}, u32[]{:S(2)}) async-start(bf16[32,24,128]{2,1,0:T(8,128)(2,1)} %bitcast.12), calls=%async_computation.2 | async-start | bytes 393216 | tf_op jit(solution)/shard_map/all_to_all | solution.py:78
  82.2 0.7 constant_dynamic-update-slice_fusion.3
  82.9 0.7 constant_dynamic-update-slice_fusion.2
  83.6 0.7 constant_dynamic-update-slice_fusion.1
  84.4 0.7 constant_dynamic-update-slice_fusion
  85.1 7.7 %all-to-all-done.2 = bf16[32,24,128]{2,1,0:T(8,128)(2,1)S(1)} async-done(((bf16[32,24,128]{2,1,0:T(8,128)(2,1)}), bf16[32,24,128]{2,1,0:T(8,128)(2,1)S(1)}, u32[]{:S(2)}, u32[]{:S(2)}) %all-to-all-start.2) | async-done | bytes 196640 | tf_op jit(solution)/shard_map/all_to_all | solution.py:78
  92.8 5.0 %all-to-all-start.4 = ((bf16[32,128,1024]{2,1,0:T(8,128)(2,1)}), bf16[32,128,1024]{2,1,0:T(8,128)(2,1)}, u32[]{:S(2)}, u32[]{:S(2)}) async-start(bf16[32,128,1024]{2,1,0:T(8,128)(2,1)} %bitcast.8), calls=%async_computation.4 | async-start | bytes 16777216 | tf_op jit(solution)/shard_map/all_to_all | solution.py:9
  98.0 0.4 convolution_multiply_fusion.1
  98.4 0.9 pad_maximum_fusion
  99.4 1.4 concatenate.21
  100.8 0.4 fusion.8
  101.2 1.5 fusion.1
  102.7 184.5 %all-to-all-done.4 = bf16[32,128,1024]{2,1,0:T(8,128)(2,1)} async-done(((bf16[32,128,1024]{2,1,0:T(8,128)(2,1)}), bf16[32,128,1024]{2,1,0:T(8,128)(2,1)}, u32[]{:S(2)}, u32[]{:S(2)}) %all-to-all-start.4) | async-done | bytes 8388640 | tf_op jit(solution)/shard_map/all_to_all | solution.py:9
  287.2 5.0 %all-to-all-start.3 = ((bf16[16,8,4608]{2,1,0:T(8,128)(2,1)}), bf16[16,8,4608]{2,1,0:T(8,128)(2,1)S(1)}, u32[]{:S(2)}, u32[]{:S(2)}) async-start(bf16[16,8,4608]{2,1,0:T(8,128)(2,1)} %fusion.1), calls=%async_computation.3 | async-start | bytes 2359296 | tf_op jit(solution)/shard_map/all_to_all | solution.py:96
  292.3 1.7 convolution_multiply_fusion
  294.0 6.0 %fusion.3 = bf16[4096,256]{1,0:T(8,128)(2,1)} fusion(f32[4096,256]{1,0:T(8,128)S(1)} %bitcast.41, bf16[4096,1024]{1,0:T(8,128)(2,1)} %bitcast.9, bf16[256,1024]{1,0:T(8,128)(2,1)} %param.10, pred[4096]{0:T(1024)(128)(4,1)S(1)} %broadcast_bitcast_fusion), kind=kOutput, calls=%fused_computation.6 | convolution fusion | flops 2150629376 | bytes 15208448 | tf_op jit(solution)/shard_map/dot_general | solution.py:97
  300.1 22.8 %all-to-all-done.3 = bf16[16,8,4608]{2,1,0:T(8,128)(2,1)S(1)} async-done(((bf16[16,8,4608]{2,1,0:T(8,128)(2,1)}), bf16[16,8,4608]{2,1,0:T(8,128)(2,1)S(1)}, u32[]{:S(2)}, u32[]{:S(2)}) %all-to-all-start.3) | async-done | bytes 1179680 | tf_op jit(solution)/shard_map/all_to_all | solution.py:96
  323.0 0.2 reshape.78
  323.2 0.6 slice.46
  323.8 0.6 slice.47
  (28 shorter events, 1.5 us)
Async XLA Ops:
  0.6 45.9 %copy-start = (bf16[4096,256]{1,0:T(8,128)(2,1)S(1)}, bf16[4096,256]{1,0:T(8,128)(2,1)}, u32[]{:S(2)}) copy-start(bf16[4096,256]{1,0:T(8,128)(2,1)} %param.8) | copy-start | bytes 6291460
  0.6 28.8 %copy-start.1 = (bf16[128,1024]{1,0:T(8,128)(2,1)S(1)}, bf16[128,1024]{1,0:T(8,128)(2,1)}, u32[]{:S(2)}) copy-start(bf16[128,1024]{1,0:T(8,128)(2,1)} %param.9) | copy-start | bytes 786436
  2.9 41.0 %all-to-all-start = ((bf16[16,8,4608]{2,1,0:T(8,128)(2,1)}), bf16[16,8,4608]{2,1,0:T(8,128)(2,1)S(1)}, u32[]{:S(2)}, u32[]{:S(2)}) async-start(bf16[16,8,4608]{2,1,0:T(8,128)(2,1)} %broadcast_in_dim.55), calls=%async_computation | async-start | bytes 2359296 | tf_op jit(solution)/shard_map/all_to_all | solution.py:47
  46.5 46.4 %copy-start.2 = (bf16[32,16,288]{2,1,0:T(8,128)(2,1)}, bf16[32,16,288]{2,1,0:T(8,128)(2,1)S(1)}, u32[]{:S(2)}) copy-start(bf16[32,16,288]{2,1,0:T(8,128)(2,1)S(1)} %reshape.67) | copy-start | bytes 884740
  48.6 24.9 %all-to-all-start.1 = ((f32[32,1,2560]{2,1,0:T(1,128)}), f32[32,1,2560]{2,1,0:T(1,128)S(1)}, u32[]{:S(2)}, u32[]{:S(2)}) async-start(f32[32,1,2560]{2,1,0:T(1,128)} %all_to_all.31), calls=%async_computation.1 | async-start | bytes 655360 | tf_op jit(solution)/shard_map/all_to_all | solution.py:56
  78.1 14.8 %all-to-all-start.2 = ((bf16[32,24,128]{2,1,0:T(8,128)(2,1)}), bf16[32,24,128]{2,1,0:T(8,128)(2,1)S(1)}, u32[]{:S(2)}, u32[]{:S(2)}) async-start(bf16[32,24,128]{2,1,0:T(8,128)(2,1)} %bitcast.12), calls=%async_computation.2 | async-start | bytes 393216 | tf_op jit(solution)/shard_map/all_to_all | solution.py:78
  92.8 194.4 %all-to-all-start.4 = ((bf16[32,128,1024]{2,1,0:T(8,128)(2,1)}), bf16[32,128,1024]{2,1,0:T(8,128)(2,1)}, u32[]{:S(2)}, u32[]{:S(2)}) async-start(bf16[32,128,1024]{2,1,0:T(8,128)(2,1)} %bitcast.8), calls=%async_computation.4 | async-start | bytes 16777216 | tf_op jit(solution)/shard_map/all_to_all | solution.py:9
  287.2 35.6 %all-to-all-start.3 = ((bf16[16,8,4608]{2,1,0:T(8,128)(2,1)}), bf16[16,8,4608]{2,1,0:T(8,128)(2,1)S(1)}, u32[]{:S(2)}, u32[]{:S(2)}) async-start(bf16[16,8,4608]{2,1,0:T(8,128)(2,1)} %fusion.1), calls=%async_computation.3 | async-start | bytes 2359296 | tf_op jit(solution)/shard_map/all_to_all | solution.py:96
